TPU v7x, 256 devices: a whole 4x4x8 slice. The times are simulated.
256 devices in a mesh: sector: 64 (over z, y, core), dof: 4 (over x).
Axes of the slice: x: 4, y: 4, z: 8, core: 2. Of those that a mesh axis runs over, the one named last changes fastest.
Arguments:
- load_history: bfloat16 [64, 64, 6144], P('sector', None, 'dof'), may hold values from -6 to 6
- sector_basis: bfloat16 [6144, 1536], P('dof'), may hold values from -0.078125 to 0.078125
- harmonic_modes: bfloat16 [64, 1536, 256], P('sector'), may hold values from -0.15625 to 0.15625
- stress_basis: bfloat16 [1536, 6144], P(None, 'dof'), may hold values from -0.375 to 0.375
- mode_decay: float32 [64, 256], P('sector'), may hold values from 0.01 to 0.3
- mode_phase: float32 [64, 256], P('sector'), may hold values from 0.05 to 1.5
- mode_count: int32 [64], P('sector'), may hold values from 64 to 256, as said below
- slot_harmonic: int32 [64], replicated, may hold values from 0 to 63, each once
Outputs:
- stress_field: bfloat16 [64, 64, 6144], P('sector', None, 'dof')
Inputs may be any that keep to these rules, and one draw needn't show every extreme that they name: Slot modes from mode_count on are left out; some slot has 256 live modes and some 256 // 4. `slot_harmonic`: every harmonic component is held by exactly one slot.
All inputs are finite; a program needn't handle non-finite values.
Results may differ from a plain program's by a relative error of at most 0.025.
Values may be sent and summed in bfloat16 or wider, within the bound.
No kernel may reach another device: no remote copies, remote signals or barrier semaphores. Data moves between devices by JAX's collectives and lax.ppermute only.
A program may use at most 64 MiB of HBM per device.

v0:
```python
import math
import jax
import jax.numpy as jnp
from jax import lax
from jax.sharding import PartitionSpec as P


def transform_table(slot_harmonic):
    count_all = slot_harmonic.shape[0]
    half_count = count_all // 2
    sine_rows = slot_harmonic > half_count
    harmonic_order = jnp.where(sine_rows, slot_harmonic - half_count, slot_harmonic)
    sector_index = jnp.arange(count_all, dtype=jnp.int32)
    residue = harmonic_order[:, None] * sector_index[None, :] % count_all
    phase_angle = residue.astype(jnp.float32) * jnp.float32(2.0 * math.pi / count_all)
    wave_table = jnp.where(sine_rows[:, None], jnp.sin(phase_angle), jnp.cos(phase_angle))
    single = (slot_harmonic == 0) | (slot_harmonic == half_count)
    weight = jnp.where(single, jnp.float32(1.0 / count_all), jnp.float32(2.0 / count_all))
    return jnp.sqrt(weight)[:, None] * wave_table


def filter_kernel(decay_rates, phase_steps, steps_count):
    time_index = jnp.arange(steps_count, dtype=jnp.int32)
    offset = time_index[:, None] - time_index[None, :]
    causal = offset >= 0
    lag_value = jnp.maximum(offset, 0).astype(jnp.float32)
    gain_factor = jnp.sqrt(1.0 - jnp.exp(-2.0 * decay_rates))
    shape_table = (
        gain_factor[..., None, None]
        * jnp.exp(-decay_rates[..., None, None] * lag_value)
        * jnp.cos(phase_steps[..., None, None] * lag_value)
    )
    return jnp.where(causal, shape_table, jnp.float32(0.0))


def local(
    load_history,
    sector_basis,
    harmonic_modes,
    stress_basis,
    mode_decay,
    mode_phase,
    mode_count,
    slot_harmonic,
):
    highest = lax.Precision.HIGHEST
    table = transform_table(slot_harmonic)
    steps_count = load_history.shape[1]
    modes_slot = harmonic_modes[0]
    partial_value = jnp.dot(load_history[0], sector_basis, preferred_element_type=jnp.float32)
    live = (jnp.arange(modes_slot.shape[1], dtype=jnp.int32) < mode_count[0]).astype(jnp.float32)
    kernel = filter_kernel(mode_decay[0], mode_phase[0], steps_count)
    reduced = lax.psum(partial_value.astype(jnp.bfloat16), "dof")
    mixed = jnp.einsum(
        "ks,stc->ktc",
        table,
        lax.all_to_all(reduced[None], "sector", split_axis=1, concat_axis=0, tiled=True).astype(
            jnp.float32
        ),
        precision=highest,
    )
    spectrum = lax.all_to_all(
        mixed.astype(jnp.bfloat16), "sector", split_axis=0, concat_axis=1, tiled=True
    )[0]
    modal = jnp.dot(spectrum, modes_slot, preferred_element_type=jnp.float32) * live[None, :]
    response = jnp.einsum("mtu,um->tm", kernel, modal, precision=highest)
    project_response = response.astype(jnp.bfloat16)
    product = lax.dot_general(
        project_response, modes_slot, (((1,), (1,)), ((), ())), preferred_element_type=jnp.float32
    )
    returned = product.astype(jnp.bfloat16)
    mixed = jnp.einsum(
        "ks,ktc->stc",
        table,
        lax.all_to_all(returned[None], "sector", split_axis=1, concat_axis=0, tiled=True).astype(
            jnp.float32
        ),
        precision=highest,
    )
    back = lax.all_to_all(
        mixed.astype(jnp.bfloat16), "sector", split_axis=0, concat_axis=1, tiled=True
    )[0]
    stress_field = jnp.dot(back, stress_basis, preferred_element_type=jnp.float32).astype(
        jnp.bfloat16
    )
    return stress_field[None]


def solution(mesh):
    return jax.shard_map(
        local,
        mesh=mesh,
        in_specs=(
            P("sector", None, "dof"),
            P("dof", None),
            P("sector", None, None),
            P(None, "dof"),
            P("sector", None),
            P("sector", None),
            P("sector"),
            P(),
        ),
        out_specs=P("sector", None, "dof"),
        check_vma=False,
    )
```

profile of v0, /device:TPU:1, one launch (start us, length us, event | category | flops | bytes accessed | tf_op | source)
XLA Modules:
  0.0 171.5 jit_solution(9315487925137367451)
XLA Ops:
  6.5 4.1 %fusion.3 = bf16[1,64,1536]{2,1,0:T(8,128)(2,1)} fusion(bf16[1536,1536]{1,0:T(8,128)(2,1)} %param.9, bf16[1,64,1536]{2,1,0:T(8,128)(2,1)} %param.8), kind=kOutput, calls=%fused_computation.9 | convolution fusion | flops 302088192 | bytes 5111808 | tf_op jit(solution)/shard_map/dot_general | solution.py:50
  10.7 48.4 %all-reduce.2.cloned.1.call-done = bf16[1,64,1536]{2,1,0:T(8,128)(2,1)} async-done(((bf16[1,64,1536]{2,1,0:T(8,128)(2,1)}), bf16[1,64,1536]{2,1,0:T(8,128)(2,1)}) %all-reduce.2.cloned.1.call-update) | async-done | bytes 196624 | tf_op jit(solution)/shard_map/psum | solution.py:53
  59.1 1.2 copy.52
  60.3 0.6 broadcast.55
  60.9 1.8 %reduce.2 = bf16[64,1536]{1,0:T(8,128)(2,1)S(1)} reduce(bf16[64,1,1536]{2,1,0:T(2,128)(2,1)S(1)} %bitcast.50, bf16[]{:T(256)} %broadcast.55), dimensions={1}, to_apply=%bitcast.48.reduce_sub_computation | reduce | bytes 393218
  62.8 0.7 reshape.75
  63.5 12.8 %all-to-all-start = ((bf16[64,2,768]{2,1,0:T(2,128)(2,1)}), bf16[64,2,768]{2,1,0:T(2,128)(2,1)S(1)}, u32[]{:S(2)}, u32[]{:S(2)}) async-start(bf16[64,2,768]{2,1,0:T(2,128)(2,1)} %reshape.75), calls=%async_computation | async-start | bytes 393216 | tf_op jit(solution)/shard_map/all_to_all | solution.py:57
  77.0 11.3 %all-to-all-done = bf16[64,2,768]{2,1,0:T(2,128)(2,1)S(1)} async-done(((bf16[64,2,768]{2,1,0:T(2,128)(2,1)}), bf16[64,2,768]{2,1,0:T(2,128)(2,1)S(1)}, u32[]{:S(2)}, u32[]{:S(2)}) %all-to-all-start) | async-done | bytes 196640 | tf_op jit(solution)/shard_map/all_to_all | solution.py:57
  88.3 0.1 reshape.76
  88.5 0.5 fusion
  89.0 0.8 reduce.3
  89.8 0.7 reshape.77
  90.5 4.5 %all-to-all-start.1 = ((bf16[64,2,768]{2,1,0:T(2,128)(2,1)}), bf16[64,2,768]{2,1,0:T(2,128)(2,1)S(1)}, u32[]{:S(2)}, u32[]{:S(2)}) async-start(bf16[64,2,768]{2,1,0:T(2,128)(2,1)} %reshape.77), calls=%async_computation.1 | async-start | bytes 393216 | tf_op jit(solution)/shard_map/all_to_all | solution.py:62
  95.0 12.1 %all-to-all-done.1 = bf16[64,2,768]{2,1,0:T(2,128)(2,1)S(1)} async-done(((bf16[64,2,768]{2,1,0:T(2,128)(2,1)}), bf16[64,2,768]{2,1,0:T(2,128)(2,1)S(1)}, u32[]{:S(2)}, u32[]{:S(2)}) %all-to-all-start.1) | async-done | bytes 196640 | tf_op jit(solution)/shard_map/all_to_all | solution.py:62
  107.2 0.2 fusion.5
  107.5 16.2 %multiply_reduce_fusion = bf16[256,64]{0,1:T(8,128)(2,1)S(1)} fusion(f32[256,64]{0,1:T(8,128)S(1)} %fusion.5, f32[256]{0:T(256)S(1)} %bitcast.56, f32[64,64]{1,0:T(8,128)S(1)} %maximum_convert_fusion, f32[256]{0:T(256)S(1)} %bitcast.55, f32[256]{0:T(256)S(1)} %bitcast.54, pred[64,64]{1,0:T(8,128)(4,1)S(1)} %fusion.21), kind=kLoop, calls=%fused_computation | loop fusion | flops 7323648 | bytes 121856
  123.9 0.4 fusion.1
  124.2 0.3 copy.51
  124.6 1.8 %reduce.4 = bf16[64,1536]{1,0:T(8,128)(2,1)S(1)} reduce(bf16[64,1,1536]{2,1,0:T(2,128)(2,1)S(1)} %bitcast.51, bf16[]{:T(256)} %broadcast.55), dimensions={1}, to_apply=%bitcast.47.reduce_sub_computation | reduce | bytes 393218
  126.5 16.2 %all_to_all.16 = bf16[64,2,768]{2,1,0:T(2,128)(2,1)S(1)} all-to-all(bf16[64,2,768]{2,1,0:T(2,128)(2,1)S(1)} %reshape.79), channel_id=1, replica_groups=mesh['sector'=64,'dof'=4] {'sector'}, dimensions={0} | all-to-all | bytes 393216 | tf_op jit(solution)/shard_map/all_to_all | solution.py:75
  142.8 0.6 fusion.2
  143.4 0.8 reduce.5
  144.3 16.3 %all_to_all.17 = bf16[64,2,768]{2,1,0:T(2,128)(2,1)S(1)} all-to-all(bf16[64,2,768]{2,1,0:T(2,128)(2,1)S(1)} %reshape.81), channel_id=1, replica_groups=mesh['sector'=64,'dof'=4] {'sector'}, dimensions={0} | all-to-all | bytes 393216 | tf_op jit(solution)/shard_map/all_to_all | solution.py:80
  160.7 3.9 %fusion.4 = bf16[1,64,1536]{2,1,0:T(8,128)(2,1)} fusion(bf16[1536,1536]{1,0:T(8,128)(2,1)} %param.11, bf16[64,1,1536]{2,1,0:T(2,128)(2,1)S(1)} %reshape.82), kind=kOutput, calls=%fused_computation.10 | convolution fusion | flops 302088192 | bytes 5111808 | tf_op jit(solution)/shard_map/dot_general | solution.py:83
  (23 shorter events, 0.7 us)
Async XLA Ops:
  6.5 100.7 %copy-start = (bf16[1,1536,256]{2,1,0:T(8,128)(2,1)S(1)}, bf16[1,1536,256]{2,1,0:T(8,128)(2,1)}, u32[]{:S(2)}) copy-start(bf16[1,1536,256]{2,1,0:T(8,128)(2,1)} %param.10) | copy-start | bytes 2359300
  6.5 4.2 %copy-start.3 = (s32[64]{0:T(128)S(1)}, s32[64]{0:T(128)}, u32[]{:S(2)}) copy-start(s32[64]{0:T(128)} %param.15) | copy-start | bytes 772
  6.5 88.4 %copy-start.1 = (f32[1,256]{1,0:T(1,128)S(1)}, f32[1,256]{1,0:T(1,128)}, u32[]{:S(2)}) copy-start(f32[1,256]{1,0:T(1,128)} %param.12) | copy-start | bytes 3076
  6.5 52.5 %all-reduce.2.cloned.1.call-start = ((), (), s32[]{:S(2)}) async-start(), calls=%async_computation.4 | async-start | bytes 393216 | tf_op jit(solution)/shard_map/psum | solution.py:53
  10.7 96.8 %copy-start.2 = (f32[1,256]{1,0:T(1,128)S(1)}, f32[1,256]{1,0:T(1,128)}, u32[]{:S(2)}) copy-start(f32[1,256]{1,0:T(1,128)} %param.13) | copy-start | bytes 3076
  63.5 24.8 %all-to-all-start = ((bf16[64,2,768]{2,1,0:T(2,128)(2,1)}), bf16[64,2,768]{2,1,0:T(2,128)(2,1)S(1)}, u32[]{:S(2)}, u32[]{:S(2)}) async-start(bf16[64,2,768]{2,1,0:T(2,128)(2,1)} %reshape.75), calls=%async_computation | async-start | bytes 393216 | tf_op jit(solution)/shard_map/all_to_all | solution.py:57
  90.5 16.6 %all-to-all-start.1 = ((bf16[64,2,768]{2,1,0:T(2,128)(2,1)}), bf16[64,2,768]{2,1,0:T(2,128)(2,1)S(1)}, u32[]{:S(2)}, u32[]{:S(2)}) async-start(bf16[64,2,768]{2,1,0:T(2,128)(2,1)} %reshape.77), calls=%async_computation.1 | async-start | bytes 393216 | tf_op jit(solution)/shard_map/all_to_all | solution.py:62
Sparse Core Ops, SparseCore 0:
  10.8 48.2 all-reduce.1
where the time goes:
time: 172 us; the launch traced here: 171 us
  waiting for transfers between devices  71.8 us (42%)
  blocking collectives  32.5 us (19%)
  other arithmetic  21.5 us (12%)
  starting transfers between devices  17.3 us (10%)
  between operations  14.2 us (8%)
  matrix products  9.72 us (6%)
  local copies, waits for them, and re-layouts  4.4 us (3%)
    psum x1, waiting for transfers between devices, local(): reduced = lax.psum(partial_value.astype(jnp.bfloat16), 'dof')  48.4 us
    unnamed x3, other arithmetic  19.9 us
    all_to_all x1, blocking collectives, local(): lax.all_to_all(mixed.astype(jnp.bfloat16), 'sector', split_axis=0, concat...  16.3 us
    all_to_all x1, blocking collectives, local(): lax.all_to_all(returned[None], 'sector', split_axis=1, concat_axis=0, til...  16.2 us
    all_to_all x1, starting transfers between devices, local(): lax.all_to_all(reduced[None], 'sector', split_axis=1, concat_axis=0, tile...  12.8 us
    all_to_all x1, waiting for transfers between devices, local(): lax.all_to_all(mixed.astype(jnp.bfloat16), 'sector', split_axis=0, concat...  12.1 us
    all_to_all x1, waiting for transfers between devices, local(): lax.all_to_all(reduced[None], 'sector', split_axis=1, concat_axis=0, tile...  11.3 us
    all_to_all x1, starting transfers between devices, local(): lax.all_to_all(mixed.astype(jnp.bfloat16), 'sector', split_axis=0, concat...  4.47 us
  transfers between devices with their start and end apart: 3, of which 3 were waited for; matrix products, arithmetic and copies ran while one was open for 0% of the time, Pallas kernels for 0%

commit v1 on v0

--- a/solution.py
+++ b/solution.py
@@ -3,6 +3,7 @@
 import jax.numpy as jnp
 from jax import lax
 from jax.sharding import PartitionSpec as P
+from jax.lax import all_gather
 
 
 def transform_table(slot_harmonic):
@@ -50,7 +51,8 @@
     partial_value = jnp.dot(load_history[0], sector_basis, preferred_element_type=jnp.float32)
     live = (jnp.arange(modes_slot.shape[1], dtype=jnp.int32) < mode_count[0]).astype(jnp.float32)
     kernel = filter_kernel(mode_decay[0], mode_phase[0], steps_count)
-    reduced = lax.psum(partial_value.astype(jnp.bfloat16), "dof")
+    track_the_goods = lambda piece_in, mesh_name: all_gather(piece_in, mesh_name).sum(axis=0)
+    reduced = track_the_goods(partial_value.astype(jnp.bfloat16), "dof")
     mixed = jnp.einsum(
         "ks,stc->ktc",
         table,

time: 172 us -> 123 us (0.72)
  waiting for transfers between devices: 71.8 us -> 23.5 us
  between operations: 14.2 us -> 0.87 us
  blocking collectives: 32.5 us -> 45.4 us
    psum x1 -> x0, waiting for transfers between devices: 48.4 us -> none  [local(): reduced = lax.psum(partial_value.astype(jnp.bfloat16), 'dof')]
    all_gather x0 -> x1, blocking collectives: none -> 12.9 us  [local(): all_gather(piece_in, mesh_name).sum(axis=0)]
  transfers between devices with their start and end apart: 3 -> 2, of which waited for: 3 -> 2; matrix products, arithmetic and copies ran while one was open for 0% -> 0% of each run, Pallas kernels for 0% -> 0%
where the time goes in v1:
time: 123 us; the launch traced here: 122 us
  blocking collectives  45.4 us (37%)
  waiting for transfers between devices  23.5 us (19%)
  other arithmetic  21.6 us (18%)
  starting transfers between devices  18.3 us (15%)
  matrix products  9.05 us (7%)
  local copies, waits for them, and re-layouts  3.48 us (3%)
    unnamed x3, other arithmetic  19.9 us
    all_to_all x1, blocking collectives, local(): lax.all_to_all(mixed.astype(jnp.bfloat16), 'sector', split_axis=0, concat...  16.3 us
    all_to_all x1, blocking collectives, local(): lax.all_to_all(returned[None], 'sector', split_axis=1, concat_axis=0, til...  16.2 us
    all_to_all x1, starting transfers between devices, local(): lax.all_to_all(reduced[None], 'sector', split_axis=1, concat_axis=0, tile...  13.9 us
    all_gather x1, blocking collectives, local(): all_gather(piece_in, mesh_name).sum(axis=0)  12.9 us
    all_to_all x1, waiting for transfers between devices, local(): lax.all_to_all(mixed.astype(jnp.bfloat16), 'sector', split_axis=0, concat...  12.2 us
    all_to_all x1, waiting for transfers between devices, local(): lax.all_to_all(reduced[None], 'sector', split_axis=1, concat_axis=0, tile...  11.3 us
    all_to_all x1, starting transfers between devices, local(): lax.all_to_all(mixed.astype(jnp.bfloat16), 'sector', split_axis=0, concat...  4.47 us
  transfers between devices with their start and end apart: 2, of which 2 were waited for; matrix products, arithmetic and copies ran while one was open for 0% of the time, Pallas kernels for 0%

profile of v1, /device:TPU:1, one launch (start us, length us, event | category | flops | bytes accessed | tf_op | source)
XLA Modules:
  0.0 122.3 jit_solution(10813655550373398990)
XLA Ops:
  0.0 3.4 %convolution_convert_fusion.4 = bf16[64,1536]{1,0:T(8,128)(2,1)S(1)} fusion(bf16[1536,1536]{1,0:T(8,128)(2,1)} %param.9, bf16[1,64,1536]{2,1,0:T(8,128)(2,1)} %param.8), kind=kOutput, calls=%fused_computation.5 | convolution fusion | flops 302088192 | bytes 5111808 | tf_op jit(solution)/shard_map/dot_general | solution.py:51
  3.5 12.9 %all-gather = bf16[256,1536]{1,0:T(8,128)(2,1)S(1)} all-gather(bf16[64,1536]{1,0:T(8,128)(2,1)S(1)} %convolution_convert_fusion.4), channel_id=2, replica_groups=mesh['sector'=64,'dof'=4] {'dof'}, dimensions={0}, use_global_device_ids=true | all-gather | bytes 983040 | tf_op jit(solution)/shard_map/all_gather | solution.py:54
  16.5 0.3 copy.51
  16.9 0.6 broadcast.55
  17.5 1.8 %reduce.3 = bf16[64,1536]{1,0:T(8,128)(2,1)S(1)} reduce(bf16[64,1,1536]{2,1,0:T(2,128)(2,1)S(1)} %bitcast.51, bf16[]{:T(256)} %broadcast.55), dimensions={1}, to_apply=%bitcast.48.reduce_sub_computation | reduce | bytes 393218
  19.3 0.7 reshape.76
  20.0 13.9 %all-to-all-start = ((bf16[64,2,768]{2,1,0:T(2,128)(2,1)}), bf16[64,2,768]{2,1,0:T(2,128)(2,1)S(1)}, u32[]{:S(2)}, u32[]{:S(2)}) async-start(bf16[64,2,768]{2,1,0:T(2,128)(2,1)} %reshape.76), calls=%async_computation | async-start | bytes 393216 | tf_op jit(solution)/shard_map/all_to_all | solution.py:59
  34.6 11.3 %all-to-all-done = bf16[64,2,768]{2,1,0:T(2,128)(2,1)S(1)} async-done(((bf16[64,2,768]{2,1,0:T(2,128)(2,1)}), bf16[64,2,768]{2,1,0:T(2,128)(2,1)S(1)}, u32[]{:S(2)}, u32[]{:S(2)}) %all-to-all-start) | async-done | bytes 196640 | tf_op jit(solution)/shard_map/all_to_all | solution.py:59
  46.1 0.5 fusion
  46.6 0.8 reduce.4
  47.4 0.7 reshape.78
  48.1 4.5 %all-to-all-start.1 = ((bf16[64,2,768]{2,1,0:T(2,128)(2,1)}), bf16[64,2,768]{2,1,0:T(2,128)(2,1)S(1)}, u32[]{:S(2)}, u32[]{:S(2)}) async-start(bf16[64,2,768]{2,1,0:T(2,128)(2,1)} %reshape.78), calls=%async_computation.1 | async-start | bytes 393216 | tf_op jit(solution)/shard_map/all_to_all | solution.py:64
  52.6 12.2 %all-to-all-done.1 = bf16[64,2,768]{2,1,0:T(2,128)(2,1)S(1)} async-done(((bf16[64,2,768]{2,1,0:T(2,128)(2,1)}), bf16[64,2,768]{2,1,0:T(2,128)(2,1)S(1)}, u32[]{:S(2)}, u32[]{:S(2)}) %all-to-all-start.1) | async-done | bytes 196640 | tf_op jit(solution)/shard_map/all_to_all | solution.py:64
  65.0 0.2 fusion.4
  65.2 16.2 %multiply_reduce_fusion = bf16[256,64]{0,1:T(8,128)(2,1)S(1)} fusion(f32[256,64]{0,1:T(8,128)S(1)} %fusion.4, f32[256]{0:T(256)S(1)} %bitcast.58, f32[64,64]{1,0:T(8,128)S(1)} %maximum_convert_fusion, f32[256]{0:T(256)S(1)} %bitcast.57, f32[256]{0:T(256)S(1)} %bitcast.56, pred[64,64]{1,0:T(8,128)(4,1)S(1)} %fusion.20), kind=kLoop, calls=%fused_computation | loop fusion | flops 7323648 | bytes 121856
  81.6 0.4 fusion.1
  81.9 0.3 copy.50
  82.3 1.8 %reduce.5 = bf16[64,1536]{1,0:T(8,128)(2,1)S(1)} reduce(bf16[64,1,1536]{2,1,0:T(2,128)(2,1)S(1)} %bitcast.52, bf16[]{:T(256)} %broadcast.55), dimensions={1}, to_apply=%bitcast.47.reduce_sub_computation | reduce | bytes 393218
  84.2 16.2 %all_to_all.16 = bf16[64,2,768]{2,1,0:T(2,128)(2,1)S(1)} all-to-all(bf16[64,2,768]{2,1,0:T(2,128)(2,1)S(1)} %reshape.80), channel_id=1, replica_groups=mesh['sector'=64,'dof'=4] {'sector'}, dimensions={0} | all-to-all | bytes 393216 | tf_op jit(solution)/shard_map/all_to_all | solution.py:77
  100.5 0.6 fusion.2
  101.1 0.8 reduce.6
  101.9 16.3 %all_to_all.17 = bf16[64,2,768]{2,1,0:T(2,128)(2,1)S(1)} all-to-all(bf16[64,2,768]{2,1,0:T(2,128)(2,1)S(1)} %reshape.82), channel_id=1, replica_groups=mesh['sector'=64,'dof'=4] {'sector'}, dimensions={0} | all-to-all | bytes 393216 | tf_op jit(solution)/shard_map/all_to_all | solution.py:82
  118.2 0.1 reshape.83
  118.3 3.9 %fusion.3 = bf16[1,64,1536]{2,1,0:T(8,128)(2,1)} fusion(bf16[1536,1536]{1,0:T(8,128)(2,1)} %param.11, bf16[64,1,1536]{2,1,0:T(2,128)(2,1)S(1)} %reshape.83), kind=kOutput, calls=%fused_computation.9 | convolution fusion | flops 302088192 | bytes 5111808 | tf_op jit(solution)/shard_map/dot_general | solution.py:85
  (22 shorter events, 0.9 us)
Async XLA Ops:
  0.0 64.9 %copy-start = (bf16[1,1536,256]{2,1,0:T(8,128)(2,1)S(1)}, bf16[1,1536,256]{2,1,0:T(8,128)(2,1)}, u32[]{:S(2)}) copy-start(bf16[1,1536,256]{2,1,0:T(8,128)(2,1)} %param.10) | copy-start | bytes 2359300
  0.0 33.9 %copy-start.3 = (s32[64]{0:T(128)S(1)}, s32[64]{0:T(128)}, u32[]{:S(2)}) copy-start(s32[64]{0:T(128)} %param.15) | copy-start | bytes 772
  3.5 49.2 %copy-start.1 = (f32[1,256]{1,0:T(1,128)S(1)}, f32[1,256]{1,0:T(1,128)}, u32[]{:S(2)}) copy-start(f32[1,256]{1,0:T(1,128)} %param.12) | copy-start | bytes 3076
  3.5 61.7 %copy-start.2 = (f32[1,256]{1,0:T(1,128)S(1)}, f32[1,256]{1,0:T(1,128)}, u32[]{:S(2)}) copy-start(f32[1,256]{1,0:T(1,128)} %param.13) | copy-start | bytes 3076
  20.0 25.9 %all-to-all-start = ((bf16[64,2,768]{2,1,0:T(2,128)(2,1)}), bf16[64,2,768]{2,1,0:T(2,128)(2,1)S(1)}, u32[]{:S(2)}, u32[]{:S(2)}) async-start(bf16[64,2,768]{2,1,0:T(2,128)(2,1)} %reshape.76), calls=%async_computation | async-start | bytes 393216 | tf_op jit(solution)/shard_map/all_to_all | solution.py:59
  48.1 16.7 %all-to-all-start.1 = ((bf16[64,2,768]{2,1,0:T(2,128)(2,1)}), bf16[64,2,768]{2,1,0:T(2,128)(2,1)S(1)}, u32[]{:S(2)}, u32[]{:S(2)}) async-start(bf16[64,2,768]{2,1,0:T(2,128)(2,1)} %reshape.78), calls=%async_computation.1 | async-start | bytes 393216 | tf_op jit(solution)/shard_map/all_to_all | solution.py:64
